TPU v7x, 256 devices: a whole 4x4x8 slice. The times are simulated.
256 devices in a mesh: slab: 64 (over z_hi, x, y), rep: 4 (over z_lo, core).
Axes of the slice: x: 4, y: 4, z: 8 (z_hi: 4, z_lo: 2; z = z_hi * 2 + z_lo), core: 2. Of those that a mesh axis runs over, the one named last changes fastest.
Arguments:
- volume: float32 [2048, 128, 1024], P('slab', 'rep'), may hold values from -6 to 6
- slices_x: bfloat16 [2048, 128, 128], P('slab', 'rep'), may hold values from -6 to 6
- slices_y: bfloat16 [2048, 16, 1024], P('slab'), may hold values from -6 to 6
- slices_z: bfloat16 [256, 128, 1024], P('slab', 'rep'), may hold values from -6 to 6
- profiles: float32 [4, 16, 128], replicated, may hold values from -1 to 2
- profile_index: int32 [25], replicated, may hold values from 0 to 3
- block_shift: int32 [25], replicated, may hold values from 0 to 7
Outputs:
- updated: float32 [2048, 128, 1024], P('slab', 'rep')
All inputs are finite; a program needn't handle non-finite values.
Results may differ from a plain program's by a relative error of at most 0.0044.
Values may be sent and summed in bfloat16 or wider, within the bound.
No kernel may reach another device: no remote copies, remote signals or barrier semaphores. Data moves between devices by JAX's collectives and lax.ppermute only.
A program may use at most 64 MiB of HBM per device.

v0:
```python
import jax
import jax.numpy as jnp
from jax import lax
from jax.sharding import Mesh, PartitionSpec as P

BLOCK = 128
SLICES = 16
step_size = 0.5


def block_mats(profiles, profile_index, block_shift):
    kinds = profiles.shape[0]
    span = profiles.shape[2]
    onehot = (profile_index[:, None] == jnp.arange(kinds, dtype=jnp.int32)[None, :]).astype(
        jnp.float32
    )
    picked = jnp.einsum("bk,ksl->bsl", onehot, profiles, precision=lax.Precision.HIGHEST)
    columns = jnp.arange(span, dtype=jnp.int32)
    target = (columns[None, :] + block_shift[:, None]) % span
    moving = (target[:, :, None] == columns[None, None, :]).astype(jnp.float32)
    shifted = jnp.einsum("bsj,bjl->bsl", picked, moving, precision=lax.Precision.HIGHEST)
    return shifted.astype(jnp.bfloat16)


def banded_matrix(along):
    count = along.shape[0]
    identity = jnp.eye(count, dtype=jnp.bfloat16)
    return (along[:, :, None, :] * identity[:, None, :, None]).reshape(
        count * SLICES, count * BLOCK
    )


def shards(volume, slices_x, slices_y, slices_z, profiles, profile_index, block_shift):
    planes, rows_here, width = volume.shape
    count_x = width // BLOCK
    count_y = slices_y.shape[1] // SLICES
    mats = block_mats(profiles, profile_index, block_shift)
    along_x = mats[:count_x]
    along_y = mats[count_x : count_x + count_y]
    along_z = mats[count_x + count_y :]
    coarse = volume.astype(jnp.bfloat16)
    banded_x = banded_matrix(along_x)
    flat_coarse = coarse.reshape(planes * rows_here, width)
    fwd_x = lax.dot_general(
        flat_coarse, banded_x, (((1,), (1,)), ((), ())), preferred_element_type=jnp.float32
    )
    resid_x = (
        slices_x.reshape(planes * rows_here, count_x * SLICES).astype(jnp.float32) - fwd_x
    ).astype(jnp.bfloat16)
    corr_x = jnp.dot(resid_x, banded_x, preferred_element_type=jnp.float32).reshape(
        planes, rows_here, width
    )
    rep = lax.axis_index("rep")
    nrep = lax.axis_size("rep")
    band_y = lax.dynamic_slice_in_dim(along_y[0], rep * rows_here, rows_here, 1)
    partial_y = jnp.einsum("sl,zlx->zsx", band_y, coarse, preferred_element_type=jnp.float32)
    fwd_y = lax.psum_scatter(partial_y, "rep", scatter_dimension=0, tiled=True)
    part_z = planes // nrep
    obs_y = lax.dynamic_slice_in_dim(slices_y, rep * part_z, part_z, 0)
    resid_y = (obs_y.astype(jnp.float32) - fwd_y).astype(jnp.bfloat16)
    resid_y = lax.all_gather(resid_y, "rep", axis=0, tiled=True)
    corr_y = jnp.einsum("sl,zsx->zlx", band_y, resid_y, preferred_element_type=jnp.float32)
    zb = lax.axis_index("zb")
    zq = lax.axis_index("zq")
    mat_z = lax.dynamic_index_in_dim(along_z, zb, 0, keepdims=False)
    band_z = lax.dynamic_slice_in_dim(mat_z, zq * planes, planes, 1)
    partial_z = jnp.einsum("sl,lyx->syx", band_z, coarse, preferred_element_type=jnp.float32)
    fwd_z = lax.psum_scatter(partial_z, "zq", scatter_dimension=0, tiled=True)
    resid_z = (slices_z.astype(jnp.float32) - fwd_z).astype(jnp.bfloat16)
    resid_z = lax.all_gather(resid_z, "zq", axis=0, tiled=True)
    corr_z = jnp.einsum("sl,syx->lyx", band_z, resid_z, preferred_element_type=jnp.float32)
    return volume + step_size * (corr_x + corr_y + corr_z)


def solution(mesh):
    nslab, nrep = mesh.devices.shape
    slab = ("zb", "zq")

    def run(volume, *rest):
        group = BLOCK // (volume.shape[0] // nslab)
        inner = Mesh(mesh.devices.reshape(nslab // group, group, nrep), ("zb", "zq", "rep"))
        return jax.shard_map(
            shards,
            mesh=inner,
            in_specs=(
                P(slab, "rep", None),
                P(slab, "rep", None),
                P(slab, None, None),
                P(slab, "rep", None),
                P(),
                P(),
                P(),
            ),
            out_specs=P(slab, "rep", None),
            check_vma=False,
        )(volume, *rest)

    return run
```

profile of v0, /device:TPU:1, one launch (start us, length us, event | category | flops | bytes accessed | tf_op | source)
XLA Modules:
  0.0 158.2 jit_solution(11104190824409723244)
XLA Ops:
  6.5 0.0 copy-start
  6.5 0.0 reduce-scatter.5.cloned.1.call-start
  6.5 0.7 add_select_fusion
  7.3 0.0 copy-done
  7.3 1.0 fusion.15
  8.3 1.0 fusion.8
  9.3 2.5 %convert_element_type.40 = bf16[32,32,1024]{2,1,0:T(8,128)(2,1)S(1)} convert(f32[32,32,1024]{2,1,0:T(8,128)} %param.7) | non-fusion elementwise | flops 1048576 | bytes 6291456 | tf_op jit(solution)/shard_map/convert_element_type | solution.py:41
  11.9 2.4 %fusion.3 = f32[16,32,1024]{2,0,1:T(8,128)S(1)} fusion(bf16[32,32,1024]{2,1,0:T(8,128)(2,1)S(1)} %convert_element_type.40, bf16[16,16,128]{2,1,0:T(8,128)(2,1)S(1)} %slice.14, s32[]{:T(128)S(6)} %select_n.32, s32[]{:T(128)S(6)} %select_n.34), kind=kOutput, calls=%fused_computation.4 | convolution fusion | flops 33554432 | bytes 4198408 | tf_op jit(solution)/shard_map/sl,lyx->syx/dot_general | solution.py:67
  14.2 2.5 %copy.21 = f32[16,32,1024]{2,1,0:T(8,128)} copy(f32[16,32,1024]{2,0,1:T(8,128)S(1)} %fusion.3) | data formatting | bytes 4194304 | tf_op jit(solution)/shard_map/sl,lyx->syx/dot_general | solution.py:67
  16.8 0.0 reduce-scatter.5.cloned.1.call-update
  16.8 0.0 reduce-scatter.3.cloned.1.call-start
  16.9 1.8 %convolution_bitcast_fusion = f32[32,16,1024]{2,1,0:T(8,128)} fusion(bf16[32,32,1024]{2,1,0:T(8,128)(2,1)S(1)} %convert_element_type.40, bf16[1,16,128]{2,1,0:T(8,128)(2,1)S(1)} %slice.13, s32[]{:T(128)S(6)} %select_n.30), kind=kOutput, calls=%fused_computation.8 | convolution fusion | flops 33554432 | bytes 4198404 | tf_op jit(solution)/shard_map/sl,zlx->zsx/dot_general | solution.py:56
  18.7 0.0 copy-start.3
  18.7 0.0 reduce-scatter.3.cloned.1.call-update
  18.7 0.0 copy-start.2
  18.7 0.0 all-gather.5.cloned.1.call-start
  18.8 34.2 %reduce-scatter.5.cloned.1.call-done = f32[4,32,1024]{2,1,0:T(8,128)} async-done(((f32[16,32,1024]{2,1,0:T(8,128)}), f32[4,32,1024]{2,1,0:T(8,128)}) %reduce-scatter.5.cloned.1.call-update) | async-done | bytes 524304 | tf_op jit(solution)/shard_map/reduce_scatter | solution.py:68
  53.0 0.0 copy-done.3
  53.0 1.8 %subtract_convert_fusion = bf16[4,32,1024]{2,1,0:T(8,128)(2,1)} fusion(f32[4,32,1024]{2,1,0:T(8,128)} %reduce-scatter.5.cloned.1.call-done, bf16[4,32,1024]{2,1,0:T(8,128)(2,1)S(1)} %copy-done.3), kind=kLoop, calls=%fused_computation.16 | loop fusion | flops 393216 | bytes 1048576 | tf_op jit(solution)/shard_map/convert_element_type | solution.py:69
  54.8 0.0 all-gather.5.cloned.1.call-update
  54.8 0.2 all-gather.3.cloned.1.call-start
  55.1 31.4 %reduce-scatter.3.cloned.1.call-done = f32[8,16,1024]{2,1,0:T(8,128)} async-done(((f32[32,16,1024]{2,1,0:T(8,128)}), f32[8,16,1024]{2,1,0:T(8,128)}) %reduce-scatter.3.cloned.1.call-update) | async-done | bytes 524304 | tf_op jit(solution)/shard_map/reduce_scatter | solution.py:57
  86.4 1.9 %subtract_convert_fusion.1 = bf16[8,16,1024]{2,1,0:T(8,128)(2,1)} fusion(f32[8,16,1024]{2,1,0:T(8,128)} %reduce-scatter.3.cloned.1.call-done, bf16[32,16,1024]{2,1,0:T(8,128)(2,1)} %param.9, s32[]{:T(128)S(6)} %select_n.29), kind=kLoop, calls=%fused_computation.17 | loop fusion | flops 393216 | bytes 1048580 | tf_op jit(solution)/shard_map/convert_element_type | solution.py:60
  88.3 0.0 all-gather.3.cloned.1.call-update
  88.3 0.1 broadcast_multiply_fusion
  88.4 0.8 reshape.72
  89.2 0.0 copy-done.2
  89.2 0.1 bitcast_convert_fusion
  89.3 0.2 copy.18
  89.5 0.0 copy-start.1
  89.5 0.8 fusion.7
  90.4 0.2 copy.19
  90.5 0.0 copy-done.1
  90.5 2.7 %fusion.37 = f32[32,32,1024]{2,1,0:T(8,128)} fusion(bf16[32,32,128]{2,1,0:T(8,128)(2,1)S(1)} %bitcast.50, bf16[128,1024,1]{1,0,2:T(8,128)(2,1)S(1)} %copy-done.1), kind=kOutput, calls=%fused_computation.49 | convolution fusion | flops 268435456 | bytes 4718592 | tf_op jit(solution)/shard_map/dot_general | solution.py:50
  93.2 19.7 %all-gather.5.cloned.1.call-done = bf16[16,32,1024]{2,1,0:T(8,128)(2,1)} async-done(((bf16[4,32,1024]{2,1,0:T(8,128)(2,1)}), bf16[16,32,1024]{2,1,0:T(8,128)(2,1)}) %all-gather.5.cloned.1.call-update) | async-done | bytes 1048592 | tf_op jit(solution)/shard_map/all_gather | solution.py:70
  112.9 4.1 %fusion.9 = f32[32,32,1024]{2,0,1:T(8,128)} fusion(bf16[16,32,1024]{2,1,0:T(8,128)(2,1)} %all-gather.5.cloned.1.call-done, bf16[16,16,128]{2,1,0:T(8,128)(2,1)S(1)} %slice.14, s32[]{:T(128)S(6)} %select_n.32, s32[]{:T(128)S(6)} %select_n.34), kind=kOutput, calls=%fused_computation.13 | convolution fusion | flops 33554432 | bytes 5246984 | tf_op jit(solution)/shard_map/sl,syx->lyx/dot_general | solution.py:71
  117.1 23.7 %all-gather.3.cloned.1.call-done = bf16[32,16,1024]{2,1,0:T(8,128)(2,1)} async-done(((bf16[8,16,1024]{2,1,0:T(8,128)(2,1)}), bf16[32,16,1024]{2,1,0:T(8,128)(2,1)}) %all-gather.3.cloned.1.call-update) | async-done | bytes 1048592 | tf_op jit(solution)/shard_map/all_gather | solution.py:61
  140.8 10.9 %fusion.2 = f32[32,32,1024]{2,1,0:T(8,128)} fusion(f32[32,32,1024]{2,1,0:T(8,128)} %param.7, f32[32,32,1024]{2,1,0:T(8,128)} %fusion.37, f32[32,32,1024]{2,0,1:T(8,128)} %fusion.9, bf16[32,16,1024]{2,1,0:T(8,128)(2,1)} %all-gather.3.cloned.1.call-done, bf16[1,16,128]{2,1,0:T(8,128)(2,1)S(1)} %slice.13, s32[]{:T(128)S(6)} %select_n.30), kind=kOutput, calls=%fused_computation.3 | convolution fusion | flops 37748736 | bytes 17829892 | tf_op jit(solution)/shard_map/sl,zsx->zlx/dot_general | solution.py:62
  (4 shorter events, 0.0 us)
Async XLA Ops:
  6.5 0.8 copy-start
  6.5 46.4 %reduce-scatter.5.cloned.1.call-start = ((), (), s32[]{:S(2)}) async-start(), calls=%async_computation.4 | async-start | bytes 2621440 | tf_op jit(solution)/shard_map/reduce_scatter | solution.py:68
  16.8 69.6 %reduce-scatter.3.cloned.1.call-start = ((), (), s32[]{:S(2)}) async-start(), calls=%async_computation.2 | async-start | bytes 2621440 | tf_op jit(solution)/shard_map/reduce_scatter | solution.py:57
  18.7 34.3 %copy-start.3 = (bf16[4,32,1024]{2,1,0:T(8,128)(2,1)S(1)}, bf16[4,32,1024]{2,1,0:T(8,128)(2,1)}, u32[]{:S(2)}) copy-start(bf16[4,32,1024]{2,1,0:T(8,128)(2,1)} %param.10) | copy-start | bytes 786436
  18.7 70.5 %copy-start.2 = (bf16[32,32,128]{2,1,0:T(8,128)(2,1)S(1)}, bf16[32,32,128]{2,1,0:T(8,128)(2,1)}, u32[]{:S(2)}) copy-start(bf16[32,32,128]{2,1,0:T(8,128)(2,1)} %param.8) | copy-start | bytes 786436
  18.7 94.2 %all-gather.5.cloned.1.call-start = ((), (), s32[]{:S(2)}) async-start(), calls=%async_computation.5 | async-start | bytes 1310720 | tf_op jit(solution)/shard_map/all_gather | solution.py:70
  54.8 86.0 %all-gather.3.cloned.1.call-start = ((), (), s32[]{:S(2)}) async-start(), calls=%async_computation.3 | async-start | bytes 1310720 | tf_op jit(solution)/shard_map/all_gather | solution.py:61
  89.5 1.0 copy-start.1
Sparse Core Ops, SparseCore 0:
  16.9 36.0 reduce-scatter.4
  55.5 30.8 reduce-scatter.2
  88.2 24.6 all-gather.4
  114.6 26.1 all-gather.2
where the time goes:
time: 158 us
  waiting for transfers between devices  109 us (69%)
  matrix products  24.8 us (16%)
  between operations  13.3 us (8%)
  other arithmetic  7.08 us (4%)
  local copies, waits for them, and re-layouts  3.76 us (2%)
    reduce_scatter x1, waiting for transfers between devices, shards(): fwd_z = lax.psum_scatter(partial_z, 'zq', scatter_dimension=0, tiled=True)  34.2 us
    reduce_scatter x1, waiting for transfers between devices, shards(): fwd_y = lax.psum_scatter(partial_y, 'rep', scatter_dimension=0, tiled=True)  31.4 us
    all_gather x1, waiting for transfers between devices, shards(): resid_y = lax.all_gather(resid_y, 'rep', axis=0, tiled=True)  23.7 us
    all_gather x1, waiting for transfers between devices, shards(): resid_z = lax.all_gather(resid_z, 'zq', axis=0, tiled=True)  19.7 us
    dot_general x1, matrix products, shards(): jnp.einsum('sl,zsx->zlx', band_y, resid_y, preferred_element_type=jnp.flo...  10.9 us
    dot_general x1, matrix products, shards(): jnp.einsum('sl,syx->lyx', band_z, resid_z, preferred_element_type=jnp.flo...  4.13 us
  transfers between devices with their start and end apart: 4, of which 4 were waited for; matrix products, arithmetic and copies ran while one was open for 9% of the time, Pallas kernels for 0%

commit v1 on v0

--- a/solution.py
+++ b/solution.py
@@ -58,7 +58,9 @@
     part_z = planes // nrep
     obs_y = lax.dynamic_slice_in_dim(slices_y, rep * part_z, part_z, 0)
     resid_y = (obs_y.astype(jnp.float32) - fwd_y).astype(jnp.bfloat16)
-    resid_y = lax.all_gather(resid_y, "rep", axis=0, tiled=True)
+    resid_y = jnp.concatenate(
+        lax.all_to_all(jnp.stack(lax.axis_size("rep") * [resid_y], 0), "rep", 0, 0), 0
+    )
     corr_y = jnp.einsum("sl,zsx->zlx", band_y, resid_y, preferred_element_type=jnp.float32)
     zb = lax.axis_index("zb")
     zq = lax.axis_index("zq")

time: 158 us -> 136 us (0.86); the launches traced: 158 us -> 134 us
  waiting for transfers between devices: 109 us -> 74.1 us
  local copies, waits for them, and re-layouts: 3.76 us -> 7.69 us
  starting transfers between devices: 0.31 us -> 3.91 us
  matrix products: 24.8 us -> 27.2 us
    all_gather x1 -> x0, waiting for transfers between devices: 23.7 us -> none  [shards(): resid_y = lax.all_gather(resid_y, 'rep', axis=0, tiled=True)]
    all_gather x1, waiting for transfers between devices: 19.7 us -> 8.26 us  [shards(): resid_z = lax.all_gather(resid_z, 'zq', axis=0, tiled=True)]
    all_to_all x0 -> x1, starting transfers between devices: none -> 3.82 us  [shards(): lax.all_to_all(jnp.stack(lax.axis_size('rep') * [resid_y], 0), 'rep', 0, 0)]
    convert_element_type x1, local copies, waits for them, and re-layouts: 0.2 us -> 2.03 us  [shards(): slices_x.reshape(planes * rows_here, count_x * SLICES).astype(jnp.float32)]
    dot_general x1, matrix products: 0.83 us -> 2.57 us  [shards(): lax.dot_general(flat_coarse, banded_x, (((1,), (1,)), ((), ())), preferre...]
    convert_element_type x1, other arithmetic: 0.05 us -> 1.78 us  [shards(): slices_x.reshape(planes * rows_here, count_x * SLICES).astype(jnp.float32)]
  transfers between devices with their start and end apart: 4 -> 4, of which waited for: 4 -> 3; matrix products, arithmetic and copies ran while one was open for 9% -> 17% of each run, Pallas kernels for 0% -> 0%
where the time goes in v1:
time: 136 us; the launch traced here: 134 us
  waiting for transfers between devices  74.1 us (54%)
  matrix products  27.2 us (20%)
  between operations  13.2 us (10%)
  other arithmetic  8.16 us (6%)
  local copies, waits for them, and re-layouts  7.69 us (6%)
  starting transfers between devices  3.91 us (3%)
    reduce_scatter x1, waiting for transfers between devices, shards(): fwd_z = lax.psum_scatter(partial_z, 'zq', scatter_dimension=0, tiled=True)  34.2 us
    reduce_scatter x1, waiting for transfers between devices, shards(): fwd_y = lax.psum_scatter(partial_y, 'rep', scatter_dimension=0, tiled=True)  31.6 us
    dot_general x1, matrix products, shards(): jnp.einsum('sl,zsx->zlx', band_y, resid_y, preferred_element_type=jnp.flo...  10.6 us
    all_gather x1, waiting for transfers between devices, shards(): resid_z = lax.all_gather(resid_z, 'zq', axis=0, tiled=True)  8.26 us
    dot_general x1, matrix products, shards(): jnp.einsum('sl,syx->lyx', band_z, resid_z, preferred_element_type=jnp.flo...  4.14 us
    all_to_all x1, starting transfers between devices, shards(): lax.all_to_all(jnp.stack(lax.axis_size('rep') * [resid_y], 0), 'rep', 0, 0)  3.82 us
    dot_general x1, matrix products, shards(): jnp.dot(resid_x, banded_x, preferred_element_type=jnp.float32)  3.68 us
  transfers between devices with their start and end apart: 4, of which 3 were waited for; matrix products, arithmetic and copies ran while one was open for 17% of the time, Pallas kernels for 0%

profile of v1, /device:TPU:1, one launch (start us, length us, event | category | flops | bytes accessed | tf_op | source)
XLA Modules:
  0.0 134.3 jit_solution(3003035407129895689)
XLA Ops:
  6.5 0.0 copy-start
  6.5 0.0 reduce-scatter.5.cloned.1.call-start
  6.5 0.7 add_select_fusion
  7.3 0.0 copy-done
  7.3 1.0 fusion.15
  8.3 1.0 fusion.8
  9.3 0.0 copy-start.2
  9.4 0.0 copy-start.3
  9.4 2.6 %convert_element_type.40 = bf16[32,32,1024]{2,1,0:T(8,128)(2,1)S(1)} convert(f32[32,32,1024]{2,1,0:T(8,128)} %param.7) | non-fusion elementwise | flops 1048576 | bytes 6291456 | tf_op jit(solution)/shard_map/convert_element_type | solution.py:41
  12.0 0.0 copy-done.3
  12.0 2.4 %fusion.3 = f32[16,32,1024]{2,0,1:T(8,128)S(1)} fusion(bf16[32,32,1024]{2,1,0:T(8,128)(2,1)S(1)} %convert_element_type.40, bf16[16,16,128]{2,1,0:T(8,128)(2,1)S(1)} %slice.14, s32[]{:T(128)S(6)} %select_n.32, s32[]{:T(128)S(6)} %select_n.34), kind=kOutput, calls=%fused_computation.4 | convolution fusion | flops 33554432 | bytes 4198408 | tf_op jit(solution)/shard_map/sl,lyx->syx/dot_general | solution.py:69
  14.3 2.5 %copy.21 = f32[16,32,1024]{2,1,0:T(8,128)} copy(f32[16,32,1024]{2,0,1:T(8,128)S(1)} %fusion.3) | data formatting | bytes 4194304 | tf_op jit(solution)/shard_map/sl,lyx->syx/dot_general | solution.py:69
  16.9 0.0 reduce-scatter.5.cloned.1.call-update
  16.9 0.0 reduce-scatter.3.cloned.1.call-start
  17.0 1.8 %convolution_bitcast_fusion = f32[32,16,1024]{2,1,0:T(8,128)} fusion(bf16[32,32,1024]{2,1,0:T(8,128)(2,1)S(1)} %convert_element_type.40, bf16[1,16,128]{2,1,0:T(8,128)(2,1)S(1)} %slice.13, s32[]{:T(128)S(6)} %select_n.30), kind=kOutput, calls=%fused_computation.8 | convolution fusion | flops 33554432 | bytes 4198404 | tf_op jit(solution)/shard_map/sl,zlx->zsx/dot_general | solution.py:56
  18.8 0.0 copy-start.1
  18.8 0.0 reduce-scatter.3.cloned.1.call-update
  18.8 0.0 all-gather.2.cloned.1.call-start
  18.9 34.2 %reduce-scatter.5.cloned.1.call-done = f32[4,32,1024]{2,1,0:T(8,128)} async-done(((f32[16,32,1024]{2,1,0:T(8,128)}), f32[4,32,1024]{2,1,0:T(8,128)}) %reduce-scatter.5.cloned.1.call-update) | async-done | bytes 524304 | tf_op jit(solution)/shard_map/reduce_scatter | solution.py:70
  53.1 0.0 copy-done.1
  53.1 1.8 %subtract_convert_fusion = bf16[4,32,1024]{2,1,0:T(8,128)(2,1)} fusion(f32[4,32,1024]{2,1,0:T(8,128)} %reduce-scatter.5.cloned.1.call-done, bf16[4,32,1024]{2,1,0:T(8,128)(2,1)S(1)} %copy-done.1), kind=kLoop, calls=%fused_computation.16 | loop fusion | flops 393216 | bytes 1048576 | tf_op jit(solution)/shard_map/convert_element_type | solution.py:71
  54.9 0.0 all-gather.2.cloned.1.call-update
  54.9 0.0 copy-done.2
  54.9 0.0 slice-start
  54.9 31.6 %reduce-scatter.3.cloned.1.call-done = f32[8,16,1024]{2,1,0:T(8,128)} async-done(((f32[32,16,1024]{2,1,0:T(8,128)}), f32[8,16,1024]{2,1,0:T(8,128)}) %reduce-scatter.3.cloned.1.call-update) | async-done | bytes 524304 | tf_op jit(solution)/shard_map/reduce_scatter | solution.py:57
  86.5 1.2 subtract_convert_fusion.1
  87.7 1.1 stack.2
  88.8 3.8 %all-to-all-start = ((bf16[4,8,16,1024]{3,2,1,0:T(8,128)(2,1)}), bf16[4,8,16,1024]{3,2,1,0:T(8,128)(2,1)S(1)}, u32[]{:S(2)}, u32[]{:S(2)}) async-start(bf16[4,8,16,1024]{3,2,1,0:T(8,128)(2,1)} %stack.2), calls=%async_computation.1 | async-start | bytes 2097152 | tf_op jit(solution)/shard_map/all_to_all | solution.py:62
  92.6 0.0 slice-done
  92.6 0.1 broadcast_multiply_fusion
  92.7 0.8 reshape.78
  93.6 1.8 %bitcast_convert_fusion = f32[1024,128]{1,0:T(8,128)} fusion(bf16[32,32,128]{2,1,0:T(8,128)(2,1)} %param.8), kind=kLoop, calls=%fused_computation.20 | loop fusion | flops 131072 | bytes 786432 | tf_op jit(solution)/shard_map/convert_element_type | solution.py:48
  95.3 2.0 %copy.18 = f32[1024,128]{0,1:T(8,128)} copy(f32[1024,128]{1,0:T(8,128)} %bitcast_convert_fusion) | data formatting | bytes 1048576 | tf_op jit(solution)/shard_map/convert_element_type | solution.py:48
  97.4 2.6 %fusion.7 = bf16[1024,128]{0,1:T(8,128)(2,1)} fusion(f32[1024,128]{0,1:T(8,128)} %copy.18, bf16[1024,1024]{1,0:T(8,128)(2,1)S(1)} %bitcast.49, bf16[16,8,8,128]{3,2,1,0:T(8,128)(2,1)S(1)} %bitcast.51), kind=kOutput, calls=%fused_computation.11 | convolution fusion | flops 268697600 | bytes 3145728 | tf_op jit(solution)/shard_map/dot_general | solution.py:44
  99.9 1.1 copy.19
  101.1 3.7 %fusion.37 = f32[32,32,1024]{2,1,0:T(8,128)} fusion(bf16[32,32,128]{2,1,0:T(8,128)(2,1)S(1)} %bitcast.52, bf16[128,1024,1]{1,0,2:T(8,128)(2,1)} %reshape.78), kind=kOutput, calls=%fused_computation.49 | convolution fusion | flops 268435456 | bytes 4718592 | tf_op jit(solution)/shard_map/dot_general | solution.py:50
  104.8 8.3 %all-gather.2.cloned.1.call-done = bf16[16,32,1024]{2,1,0:T(8,128)(2,1)} async-done(((bf16[4,32,1024]{2,1,0:T(8,128)(2,1)}), bf16[16,32,1024]{2,1,0:T(8,128)(2,1)}) %all-gather.2.cloned.1.call-update) | async-done | bytes 1048592 | tf_op jit(solution)/shard_map/all_gather | solution.py:72
  113.0 4.1 %fusion.9 = f32[32,32,1024]{2,0,1:T(8,128)} fusion(bf16[16,32,1024]{2,1,0:T(8,128)(2,1)} %all-gather.2.cloned.1.call-done, bf16[16,16,128]{2,1,0:T(8,128)(2,1)} %copy-done.3, s32[]{:T(128)S(6)} %select_n.32, s32[]{:T(128)S(6)} %select_n.34), kind=kOutput, calls=%fused_computation.13 | convolution fusion | flops 33554432 | bytes 5246984 | tf_op jit(solution)/shard_map/sl,syx->lyx/dot_general | solution.py:73
  117.2 0.0 all-to-all-done
  117.2 10.6 %fusion.2 = f32[32,32,1024]{2,1,0:T(8,128)} fusion(f32[32,32,1024]{2,1,0:T(8,128)} %param.7, f32[32,32,1024]{2,1,0:T(8,128)} %fusion.37, f32[32,32,1024]{2,0,1:T(8,128)} %fusion.9, bf16[32,16,1024]{2,1,0:T(8,128)(2,1)S(1)} %bitcast.50, bf16[1,16,128]{2,1,0:T(8,128)(2,1)S(1)} %slice.13, s32[]{:T(128)S(6)} %select_n.30), kind=kOutput, calls=%fused_computation.3 | convolution fusion | flops 37748736 | bytes 17829892 | tf_op jit(solution)/shard_map/sl,zsx->zlx/dot_general | solution.py:64
  (3 shorter events, 0.0 us)
Async XLA Ops:
  6.5 0.8 copy-start
  6.5 46.5 %reduce-scatter.5.cloned.1.call-start = ((), (), s32[]{:S(2)}) async-start(), calls=%async_computation.4 | async-start | bytes 2621440 | tf_op jit(solution)/shard_map/reduce_scatter | solution.py:70
  9.3 45.6 %copy-start.2 = (bf16[25,16,128]{2,1,0:T(8,128)(2,1)}, bf16[25,16,128]{2,1,0:T(8,128)(2,1)S(1)}, u32[]{:S(2)}) copy-start(bf16[25,16,128]{2,1,0:T(8,128)(2,1)S(1)} %fusion.8) | copy-start | bytes 307204
  9.4 2.6 %copy-start.3 = (bf16[16,16,128]{2,1,0:T(8,128)(2,1)}, bf16[16,16,128]{2,1,0:T(8,128)(2,1)S(1)}, u32[]{:S(2)}) copy-start(bf16[16,16,128]{2,1,0:T(8,128)(2,1)S(1)} %slice.14) | copy-start | bytes 196612
  16.9 69.6 %reduce-scatter.3.cloned.1.call-start = ((), (), s32[]{:S(2)}) async-start(), calls=%async_computation.3 | async-start | bytes 2621440 | tf_op jit(solution)/shard_map/reduce_scatter | solution.py:57
  18.8 34.3 %copy-start.1 = (bf16[4,32,1024]{2,1,0:T(8,128)(2,1)S(1)}, bf16[4,32,1024]{2,1,0:T(8,128)(2,1)}, u32[]{:S(2)}) copy-start(bf16[4,32,1024]{2,1,0:T(8,128)(2,1)} %param.10) | copy-start | bytes 786436
  18.8 94.2 %all-gather.2.cloned.1.call-start = ((), (), s32[]{:S(2)}) async-start(), calls=%async_computation.5 | async-start | bytes 1310720 | tf_op jit(solution)/shard_map/all_gather | solution.py:72
  54.9 37.7 %slice-start = ((bf16[25,16,128]{2,1,0:T(8,128)(2,1)}), bf16[8,16,128]{2,1,0:T(8,128)(2,1)S(1)}, s32[]{:S(2)}) async-start(bf16[25,16,128]{2,1,0:T(8,128)(2,1)} %copy-done.2), calls=%async_computation.6 | async-start | bytes 65536 | tf_op jit(solution)/shard_map/slice | solution.py:38
  88.8 28.4 %all-to-all-start = ((bf16[4,8,16,1024]{3,2,1,0:T(8,128)(2,1)}), bf16[4,8,16,1024]{3,2,1,0:T(8,128)(2,1)S(1)}, u32[]{:S(2)}, u32[]{:S(2)}) async-start(bf16[4,8,16,1024]{3,2,1,0:T(8,128)(2,1)} %stack.2), calls=%async_computation.1 | async-start | bytes 2097152 | tf_op jit(solution)/shard_map/all_to_all | solution.py:62
Sparse Core Ops, SparseCore 0:
  17.0 36.0 reduce-scatter.4
  55.6 30.8 reduce-scatter.2
  88.3 24.6 all-gather.1
